TPU v7x, 128 devices: a whole 4x4x4 slice. The times are simulated.
128 devices in a mesh: ctx: 32 (over x, y, core), head: 4 (over z).
Axes of the slice: x: 4, y: 4, z: 4, core: 2. Of those that a mesh axis runs over, the one named last changes fastest.
Arguments:
- queries: bfloat16 [32768, 4096], P('ctx', 'head'), may hold values from -4.5 to 4.5
- keys: bfloat16 [32768, 4096], P('ctx', 'head'), may hold values from -6 to 6
- values: bfloat16 [32768, 4096], P('ctx', 'head'), may hold values from -5.5 to 5.5
- row_target: int32 [32768], replicated, may hold values from 0 to 32767, as said below
- seg_doc: int32 [32], replicated, may hold values from 0 to 3, as said below
- mem_gate: float32 [32], P('head'), may hold values from -2 to 2
- out_weight: bfloat16 [4096, 4096], P(None, 'head'), may hold values from -0.09375 to 0.09375
Outputs:
- layer_out: bfloat16 [32768, 4096], P('ctx', 'head')
Inputs may be any that keep to these rules, and one draw needn't show every extreme that they name: `row_target`: a permutation of the token indices; the rows of one ctx shard of the loader order hold at most 48 tokens of any one segment, and exactly 48 of some. `seg_doc`: never falling along the segments, every document present with one or more segments.
All inputs are finite; a program needn't handle non-finite values.
Results may differ from a plain program's by a relative error of at most 0.0051.
Values may be sent and summed in bfloat16 or wider, within the bound.
No kernel may reach another device: no remote copies, remote signals or barrier semaphores. Data moves between devices by JAX's collectives and lax.ppermute only.
A program may use at most 128 MiB of HBM per device.

v0:
```python
import jax
import jax.numpy as jnp
from jax import lax
from jax.sharding import PartitionSpec as P


def feature(inputs):
    return jax.nn.elu(inputs) + 1.0


def per_device(queries, keys, values, row_target, seg_doc, mem_gate, out_weight):
    highest = lax.Precision.HIGHEST
    f32, bf16 = (jnp.float32, jnp.bfloat16)
    n = lax.axis_size("ctx")
    me = lax.axis_index("ctx")
    seg, width = queries.shape
    heads = mem_gate.shape[0]
    dh = width // heads
    cap = seg // n + seg // n // 2
    slots = n * cap
    targets = row_target.reshape(n, seg)
    r_idx = jnp.arange(seg, dtype=jnp.int32)
    o_idx = jnp.arange(n, dtype=jnp.int32)
    s_idx = jnp.arange(slots, dtype=jnp.int32)
    w_idx = jnp.arange(cap, dtype=jnp.int32)
    lower = (r_idx[None, :] < r_idx[:, None]).astype(bf16)
    mine = lax.dynamic_index_in_dim(targets, me, 0, keepdims=False)
    owner = mine // seg
    match = (owner[:, None] == o_idx[None, :]).astype(bf16)
    before = jnp.dot(lower, match, preferred_element_type=f32)
    within = jnp.sum(jnp.where(match > 0, before, 0.0), axis=1).astype(jnp.int32)
    send_slot = owner * cap + within
    slot_row = jnp.sum(jnp.where(send_slot[None, :] == s_idx[:, None], r_idx[None, :], 0), axis=1)
    arrived = targets // seg == me
    rank = jnp.dot(arrived.astype(bf16), lower.T, preferred_element_type=f32).astype(jnp.int32)
    hit = arrived[:, None, :] & (rank[:, None, :] == w_idx[None, :, None])
    pslot = jnp.sum(jnp.where(hit, (targets % seg)[:, None, :], 0), axis=2).reshape(slots)
    count = jnp.sum(arrived.astype(jnp.int32), axis=1)
    valid = (w_idx[None, :] < count[:, None]).reshape(slots)
    tok_slot = jnp.sum(
        jnp.where((pslot[None, :] == r_idx[:, None]) & valid[None, :], s_idx[None, :], 0), axis=1
    )
    doc = seg_doc[me]
    start = jnp.min(jnp.where(seg_doc == doc, o_idx, n))
    score_scale = dh ** (-0.5)
    causal = r_idx[:, None] >= r_idx[None, :]
    head_count = lax.axis_size("head")
    out_cols = out_weight.shape[1]
    bounds = [0, heads // 2, heads]
    weight_rows = out_weight.reshape(head_count, heads, dh, out_cols)
    gate_all = jax.nn.sigmoid(mem_gate)
    shifts = []
    step = 1
    while step < n:
        shifts.append(step)
        step *= 2

    def dispatch(source):
        buffer = jnp.take(source, slot_row, axis=0, mode="clip").reshape(n, cap, width)
        got = lax.all_to_all(buffer, "ctx", 0, 0, tiled=True).reshape(slots, width)
        return jnp.take(got, tok_slot, axis=0, mode="clip").reshape(seg, heads, dh)

    key_all = dispatch(keys)
    value_all = dispatch(values)
    query_all = dispatch(queries)

    def local_attention(query_part, key_part, value_part):
        scores = (
            jnp.einsum("qhd,khd->hqk", query_part, key_part, preferred_element_type=f32)
            * score_scale
        )
        scores = jnp.where(causal[None], scores, -1e30)
        row_max = jnp.max(scores, axis=-1, keepdims=True)
        weights = jnp.exp(scores - row_max)
        probabilities = (weights / jnp.sum(weights, axis=-1, keepdims=True)).astype(bf16)
        return jnp.einsum("hqk,khd->qhd", probabilities, value_part, preferred_element_type=f32)

    def one_group(g, hold):
        first, last = (bounds[g], bounds[g + 1])
        group_heads = last - first
        group_width = group_heads * dh
        cuts = [first + round(group_heads * i / len(shifts)) for i in range(len(shifts) + 1)]
        cuts = [c - first for c in cuts]
        key_heads = key_all[:, first:last]
        value_heads = value_all[:, first:last]
        query_heads = query_all[:, first:last]
        key_feat = feature(key_heads.astype(f32))
        delta_m = jnp.einsum("khd,khe->hde", key_feat, value_heads.astype(f32), precision=highest)
        delta_z = jnp.sum(key_feat, axis=0)
        delta = jnp.concatenate([delta_m, delta_z[:, None, :]], axis=1)
        pieces = []
        total = delta
        for k, step in enumerate(shifts):
            lo, hi = (cuts[k], cuts[k + 1])
            total, operands = lax.optimization_barrier(
                (total, (query_heads[:, lo:hi], key_heads[:, lo:hi], value_heads[:, lo:hi]))
            )
            perm = [(j, j + step) for j in range(n - step)]
            got = lax.ppermute(total, "ctx", perm)
            if hi > lo:
                piece = local_attention(*operands)
                got, piece = lax.optimization_barrier((got, piece))
                pieces.append(piece)
            total = total + jnp.where(me - step >= start, got, jnp.zeros_like(got))
        local_out = jnp.concatenate(pieces, axis=1)
        memory = total - delta
        mem_m = memory[:, :dh, :]
        mem_z = memory[:, dh, :]
        query_feat = feature(query_heads.astype(f32))
        numerator = jnp.einsum("qhd,hde->qhe", query_feat, mem_m, precision=highest)
        denominator = jnp.einsum("qhd,hd->qh", query_feat, mem_z, precision=highest)
        recalled = numerator / jnp.maximum(denominator, 1.0)[..., None]
        gate_value = gate_all[first:last][None, :, None]
        combined = (
            (gate_value * recalled + (1.0 - gate_value) * local_out)
            .astype(bf16)
            .reshape(seg, group_width)
        )
        outgoing = jnp.take(combined, pslot, axis=0, mode="clip").reshape(n, cap, group_width)
        incoming = lax.all_to_all(outgoing, "ctx", 0, 0, tiled=True).reshape(slots, group_width)
        rows = jnp.take(incoming, send_slot, axis=0, mode="clip")
        gathered = lax.all_gather(rows, "head", axis=1, tiled=True)
        part = jnp.dot(
            gathered,
            weight_rows[:, first:last].reshape(head_count * group_width, out_cols),
            preferred_element_type=f32,
        )
        return (part, combined)

    summed, hold = one_group(0, None)
    for g in range(1, len(bounds) - 1):
        part, hold = one_group(g, hold)
        summed = summed + part
    return summed.astype(bf16)


def solution(mesh):
    return jax.shard_map(
        per_device,
        mesh=mesh,
        in_specs=(
            P("ctx", "head"),
            P("ctx", "head"),
            P("ctx", "head"),
            P(),
            P(),
            P("head"),
            P(None, "head"),
        ),
        out_specs=P("ctx", "head"),
        check_vma=False,
    )
```

profile of v0, /device:TPU:1, one launch (start us, length us, event | category | flops | bytes accessed | tf_op | source)
XLA Modules:
  0.0 402.4 jit_solution(4213001769700298006)
XLA Ops:
  9.0 5.8 %gather_fusion.2 = bf16[1536,1024]{1,0:T(8,128)(2,1)} fusion(bf16[1024,1024]{1,0:T(8,128)(2,1)S(1)} %copy-done, s32[2048]{0:T(1024)S(1)} %pad_clamp_fusion.1), kind=kCustom, calls=%fused_computation.2 | custom fusion | bytes 6297600 | tf_op jit(solution)/shard_map/jit(_take)/gather | solution.py:59
  14.8 8.8 %all-to-all-start.1 = ((bf16[32,48,1024]{2,1,0:T(8,128)(2,1)}), bf16[32,48,1024]{2,1,0:T(8,128)(2,1)}, u32[]{:S(2)}, u32[]{:S(2)}) async-start(bf16[32,48,1024]{2,1,0:T(8,128)(2,1)} %bitcast.224), calls=%async_computation.1 | async-start | bytes 6291456 | tf_op jit(solution)/shard_map/all_to_all | solution.py:60
  23.6 5.8 %gather_fusion = bf16[1536,1024]{1,0:T(8,128)(2,1)} fusion(bf16[1024,1024]{1,0:T(8,128)(2,1)S(1)} %copy-done.2, s32[2048]{0:T(1024)S(1)} %pad_clamp_fusion.1), kind=kCustom, calls=%fused_computation | custom fusion | bytes 6297600 | tf_op jit(solution)/shard_map/jit(_take)/gather | solution.py:59
  29.5 34.0 %all-to-all-done.1 = bf16[32,48,1024]{2,1,0:T(8,128)(2,1)} async-done(((bf16[32,48,1024]{2,1,0:T(8,128)(2,1)}), bf16[32,48,1024]{2,1,0:T(8,128)(2,1)}, u32[]{:S(2)}, u32[]{:S(2)}) %all-to-all-start.1) | async-done | bytes 3145760 | tf_op jit(solution)/shard_map/all_to_all | solution.py:60
  71.9 5.8 %gather_fusion.4 = bf16[1536,1024]{1,0:T(8,128)(2,1)} fusion(bf16[1024,1024]{1,0:T(8,128)(2,1)S(1)} %copy-done.3, s32[2048]{0:T(1024)S(1)} %pad_clamp_fusion.1), kind=kCustom, calls=%fused_computation.4 | custom fusion | bytes 6297600 | tf_op jit(solution)/shard_map/jit(_take)/gather | solution.py:59
  79.1 29.2 %all-to-all-done = bf16[32,48,1024]{2,1,0:T(8,128)(2,1)} async-done(((bf16[32,48,1024]{2,1,0:T(8,128)(2,1)}), bf16[32,48,1024]{2,1,0:T(8,128)(2,1)}, u32[]{:S(2)}, u32[]{:S(2)}) %all-to-all-start) | async-done | bytes 3145760 | tf_op jit(solution)/shard_map/all_to_all | solution.py:60
  108.3 5.3 %all-to-all-start.2 = ((bf16[32,48,1024]{2,1,0:T(8,128)(2,1)}), bf16[32,48,1024]{2,1,0:T(8,128)(2,1)S(1)}, u32[]{:S(2)}, u32[]{:S(2)}) async-start(bf16[32,48,1024]{2,1,0:T(8,128)(2,1)} %bitcast.222), calls=%async_computation.2 | async-start | bytes 6291456 | tf_op jit(solution)/shard_map/all_to_all | solution.py:60
  118.1 8.3 %gather_fusion.3 = bf16[1024,1024]{1,0:T(8,128)(2,1)} fusion(bf16[1536,1024]{1,0:T(8,128)(2,1)} %bitcast.6, s32[1024]{0:T(1024)S(1)} %broadcast_clamp_fusion.1), kind=kCustom, calls=%fused_computation.3 | custom fusion | bytes 4198400 | tf_op jit(solution)/shard_map/jit(_take)/gather | solution.py:61
  130.4 8.3 %gather_fusion.1 = bf16[1024,1024]{1,0:T(8,128)(2,1)} fusion(bf16[1536,1024]{1,0:T(8,128)(2,1)} %bitcast.4, s32[1024]{0:T(1024)S(1)} %broadcast_clamp_fusion.1), kind=kCustom, calls=%fused_computation.1 | custom fusion | bytes 4198400 | tf_op jit(solution)/shard_map/jit(_take)/gather | solution.py:61
  155.9 5.3 %gather_fusion.5 = bf16[1024,1024]{1,0:T(8,128)(2,1)} fusion(bf16[1536,1024]{1,0:T(8,128)(2,1)S(1)} %bitcast.215, s32[1024]{0:T(1024)S(1)} %broadcast_clamp_fusion.1), kind=kCustom, calls=%fused_computation.5 | custom fusion | bytes 4198400 | tf_op jit(solution)/shard_map/jit(_take)/gather | solution.py:61
  200.6 6.2 %collective-permute-start.3 = (f32[4,129,128]{2,1,0:T(8,128)S(1)}, f32[4,129,128]{2,1,0:T(8,128)S(1)}, u32[]{:S(2)}, u32[]{:S(2)}) collective-permute-start(f32[4,129,128]{2,1,0:T(8,128)S(1)} %select_add_fusion.5), channel_id=1, source_target_pairs={{0,32},{4,36},{8,40},{12,44},{16,48},{20,52},{24,56},{28,60},{32,6... | collective-permute-start | bytes 792584 | tf_op jit(solution)/shard_map/ppermute | solution.py:99
  210.3 5.5 %collective-permute-start.4 = (f32[4,129,128]{2,1,0:T(8,128)S(1)}, f32[4,129,128]{2,1,0:T(8,128)S(1)}, u32[]{:S(2)}, u32[]{:S(2)}) collective-permute-start(f32[4,129,128]{2,1,0:T(8,128)S(1)} %select_add_fusion.4), channel_id=1, source_target_pairs={{0,64},{4,68},{8,72},{12,76},{16,80},{20,84},{24,88},{28,92},{32,9... | collective-permute-start | bytes 792584 | tf_op jit(solution)/shard_map/ppermute | solution.py:99
  227.5 5.4 %gather_fusion.6 = bf16[1536,512]{1,0:T(8,128)(2,1)} fusion(bf16[1024,512]{1,0:T(8,128)(2,1)S(1)} %copy.61, s32[2048]{0:T(1024)S(1)} %pad_clamp_fusion), kind=kCustom, calls=%fused_computation.6 | custom fusion | bytes 3151872 | tf_op jit(solution)/shard_map/jit(_take)/gather | solution.py:119
  232.9 11.0 %all-to-all-start.3 = ((bf16[32,48,512]{2,1,0:T(8,128)(2,1)}), bf16[32,48,512]{2,1,0:T(8,128)(2,1)S(1)}, u32[]{:S(2)}, u32[]{:S(2)}) async-start(bf16[32,48,512]{2,1,0:T(8,128)(2,1)} %bitcast.39), calls=%async_computation.3 | async-start | bytes 3145728 | tf_op jit(solution)/shard_map/all_to_all | solution.py:120
  249.0 6.0 %collective-permute-start.7 = (f32[4,129,128]{2,1,0:T(8,128)S(1)}, f32[4,129,128]{2,1,0:T(8,128)S(1)}, u32[]{:S(2)}, u32[]{:S(2)}) collective-permute-start(f32[4,129,128]{2,1,0:T(8,128)S(1)} %select_add_fusion.2), channel_id=1, source_target_pairs={{0,16},{4,20},{8,24},{12,28},{16,32},{20,36},{24,40},{28,44},{32,4... | collective-permute-start | bytes 792584 | tf_op jit(solution)/shard_map/ppermute | solution.py:99
  256.7 9.9 %all-to-all-done.3 = bf16[32,48,512]{2,1,0:T(8,128)(2,1)S(1)} async-done(((bf16[32,48,512]{2,1,0:T(8,128)(2,1)}), bf16[32,48,512]{2,1,0:T(8,128)(2,1)S(1)}, u32[]{:S(2)}, u32[]{:S(2)}) %all-to-all-start.3) | async-done | bytes 1572896 | tf_op jit(solution)/shard_map/all_to_all | solution.py:120
  266.6 5.1 %gather_fusion.7 = bf16[1024,512]{1,0:T(8,128)(2,1)} fusion(bf16[1536,512]{1,0:T(8,128)(2,1)S(1)} %bitcast.216, s32[1024]{0:T(1024)S(1)} %broadcast_clamp_fusion), kind=kCustom, calls=%fused_computation.7 | custom fusion | bytes 2101248 | tf_op jit(solution)/shard_map/jit(_take)/gather | solution.py:121
  278.8 6.7 %collective-permute-start.9 = (f32[4,129,128]{2,1,0:T(8,128)S(1)}, f32[4,129,128]{2,1,0:T(8,128)S(1)}, u32[]{:S(2)}, u32[]{:S(2)}) collective-permute-start(f32[4,129,128]{2,1,0:T(8,128)S(1)} %select_add_fusion), channel_id=1, source_target_pairs={{0,64},{4,68},{8,72},{12,76},{16,80},{20,84},{24,88},{28,92},{32,9... | collective-permute-start | bytes 792584 | tf_op jit(solution)/shard_map/ppermute | solution.py:99
  301.4 31.2 %all_to_all.25 = bf16[32,48,512]{2,1,0:T(8,128)(2,1)S(1)} all-to-all(bf16[32,48,512]{2,1,0:T(8,128)(2,1)S(1)} %bitcast.231), channel_id=1, replica_groups=mesh['ctx'=32,'head'=4] {'ctx'}, dimensions={0} | all-to-all | bytes 3145728 | tf_op jit(solution)/shard_map/all_to_all | solution.py:120
  332.6 5.0 %gather_fusion.9 = bf16[1024,512]{1,0:T(8,128)(2,1)} fusion(bf16[1536,512]{1,0:T(8,128)(2,1)S(1)} %bitcast.217, s32[1024]{0:T(1024)S(1)} %broadcast_clamp_fusion), kind=kCustom, calls=%fused_computation.9 | custom fusion | bytes 2101248 | tf_op jit(solution)/shard_map/jit(_take)/gather | solution.py:121
  337.7 6.1 %fusion.164 = (bf16[4,4,128,1024]{3,2,1,0:T(8,128)(2,1)}, bf16[4,4,128,1024]{3,2,1,0:T(8,128)(2,1)}) fusion(bf16[4,8,128,1024]{3,2,1,0:T(8,128)(2,1)} %bitcast.227), kind=kLoop, calls=%fused_computation.258 | loop fusion | bytes 16777216 | tf_op jit(solution)/shard_map/slice | solution.py:125
  343.8 10.6 %fusion.171 = f32[1024,1024]{1,0:T(8,128)} fusion(bf16[1024,2048]{1,0:T(8,128)(2,1)} %all-gather.5.cloned.1.call-done, bf16[2048,1024]{1,0:T(8,128)(2,1)} %bitcast.233), kind=kOutput, calls=%fused_computation.265 | convolution fusion | flops 4294967296 | bytes 12582912 | tf_op jit(solution)/shard_map/dot_general | solution.py:123
  354.4 30.2 %all-gather.7.cloned.1.call-done = bf16[1024,2048]{1,0:T(8,128)(2,1)} async-done(((bf16[1024,512]{1,0:T(8,128)(2,1)}), bf16[1024,2048]{1,0:T(8,128)(2,1)}) %all-gather.7.cloned.1.call-update) | async-done | bytes 4194320 | tf_op jit(solution)/shard_map/all_gather | solution.py:122
  384.5 10.6 %add_convert_fusion = bf16[1024,1024]{1,0:T(8,128)(2,1)} fusion(f32[1024,1024]{1,0:T(8,128)} %fusion.171, bf16[1024,2048]{1,0:T(8,128)(2,1)} %all-gather.7.cloned.1.call-done, bf16[2048,1024]{1,0:T(8,128)(2,1)} %bitcast.232), kind=kOutput, calls=%fused_computation.26 | convolution fusion | flops 4297064448 | bytes 14680064 | tf_op jit(solution)/shard_map/dot_general | solution.py:123
  (179 shorter events, 118.4 us)
Async XLA Ops:
  7.6 61.5 %copy-start.16 = (s32[32,1024]{1,0:T(8,128)}, s32[32,1024]{1,0:T(8,128)S(1)}, u32[]{:S(2)}) copy-start(s32[32,1024]{1,0:T(8,128)S(1)} %reshape.467) | copy-start | bytes 393220
  14.8 48.6 %all-to-all-start.1 = ((bf16[32,48,1024]{2,1,0:T(8,128)(2,1)}), bf16[32,48,1024]{2,1,0:T(8,128)(2,1)}, u32[]{:S(2)}, u32[]{:S(2)}) async-start(bf16[32,48,1024]{2,1,0:T(8,128)(2,1)} %bitcast.224), calls=%async_computation.1 | async-start | bytes 6291456 | tf_op jit(solution)/shard_map/all_to_all | solution.py:60
  29.5 39.0 %copy-start.27 = (s32[32]{0:T(128)S(1)}, s32[32]{0:T(128)}, u32[]{:S(2)}) copy-start(s32[32]{0:T(128)} %param.11) | copy-start | bytes 388
  29.5 42.4 %copy-start.3 = (bf16[1024,1024]{1,0:T(8,128)(2,1)S(1)}, bf16[1024,1024]{1,0:T(8,128)(2,1)}, u32[]{:S(2)}) copy-start(bf16[1024,1024]{1,0:T(8,128)(2,1)} %param.7) | copy-start | bytes 6291460
  63.4 44.9 %all-to-all-start = ((bf16[32,48,1024]{2,1,0:T(8,128)(2,1)}), bf16[32,48,1024]{2,1,0:T(8,128)(2,1)}, u32[]{:S(2)}, u32[]{:S(2)}) async-start(bf16[32,48,1024]{2,1,0:T(8,128)(2,1)} %bitcast.223), calls=%async_computation | async-start | bytes 6291456 | tf_op jit(solution)/shard_map/all_to_all | solution.py:60
  108.3 47.6 %all-to-all-start.2 = ((bf16[32,48,1024]{2,1,0:T(8,128)(2,1)}), bf16[32,48,1024]{2,1,0:T(8,128)(2,1)S(1)}, u32[]{:S(2)}, u32[]{:S(2)}) async-start(bf16[32,48,1024]{2,1,0:T(8,128)(2,1)} %bitcast.222), calls=%async_computation.2 | async-start | bytes 6291456 | tf_op jit(solution)/shard_map/all_to_all | solution.py:60
  167.3 13.4 %collective-permute-start = (f32[4,129,128]{2,1,0:T(8,128)S(1)}, f32[4,129,128]{2,1,0:T(8,128)S(1)}, u32[]{:S(2)}, u32[]{:S(2)}) collective-permute-start(f32[4,129,128]{2,1,0:T(8,128)S(1)} %pad_maximum_fusion), channel_id=1, source_target_pairs={{0,4},{4,8},{8,12},{12,16},{16,20},{20,24},{24,28},{28,32},{32,36}... | collective-permute-start | bytes 792584 | tf_op jit(solution)/shard_map/ppermute | solution.py:99
  171.0 12.9 %collective-permute-start.5 = (f32[4,129,128]{2,1,0:T(8,128)S(1)}, f32[4,129,128]{2,1,0:T(8,128)S(1)}, u32[]{:S(2)}, u32[]{:S(2)}) collective-permute-start(f32[4,129,128]{2,1,0:T(8,128)S(1)} %pad_maximum_fusion.1), channel_id=1, source_target_pairs={{0,4},{4,8},{8,12},{12,16},{16,20},{20,24},{24,28},{28,32},{32,36}... | collective-permute-start | bytes 792584 | tf_op jit(solution)/shard_map/ppermute | solution.py:99
  180.7 9.6 %collective-permute-start.1 = (f32[4,129,128]{2,1,0:T(8,128)S(1)}, f32[4,129,128]{2,1,0:T(8,128)S(1)}, u32[]{:S(2)}, u32[]{:S(2)}) collective-permute-start(f32[4,129,128]{2,1,0:T(8,128)S(1)} %select_add_fusion.7), channel_id=1, source_target_pairs={{0,8},{4,12},{8,16},{12,20},{16,24},{20,28},{24,32},{28,36},{32,40... | collective-permute-start | bytes 792584 | tf_op jit(solution)/shard_map/ppermute | solution.py:99
  183.9 65.1 %collective-permute-start.6 = (f32[4,129,128]{2,1,0:T(8,128)S(1)}, f32[4,129,128]{2,1,0:T(8,128)}, u32[]{:S(2)}, u32[]{:S(2)}) collective-permute-start(f32[4,129,128]{2,1,0:T(8,128)S(1)} %select_add_fusion.3), channel_id=1, source_target_pairs={{0,8},{4,12},{8,16},{12,20},{16,24},{20,28},{24,32},{28,36},{32,40... | collective-permute-start | bytes 792584 | tf_op jit(solution)/shard_map/ppermute | solution.py:99
  190.3 10.3 %collective-permute-start.2 = (f32[4,129,128]{2,1,0:T(8,128)S(1)}, f32[4,129,128]{2,1,0:T(8,128)S(1)}, u32[]{:S(2)}, u32[]{:S(2)}) collective-permute-start(f32[4,129,128]{2,1,0:T(8,128)S(1)} %select_add_fusion.6), channel_id=1, source_target_pairs={{0,16},{4,20},{8,24},{12,28},{16,32},{20,36},{24,40},{28,44},{32,4... | collective-permute-start | bytes 792584 | tf_op jit(solution)/shard_map/ppermute | solution.py:99
  200.6 9.6 %collective-permute-start.3 = (f32[4,129,128]{2,1,0:T(8,128)S(1)}, f32[4,129,128]{2,1,0:T(8,128)S(1)}, u32[]{:S(2)}, u32[]{:S(2)}) collective-permute-start(f32[4,129,128]{2,1,0:T(8,128)S(1)} %select_add_fusion.5), channel_id=1, source_target_pairs={{0,32},{4,36},{8,40},{12,44},{16,48},{20,52},{24,56},{28,60},{32,6... | collective-permute-start | bytes 792584 | tf_op jit(solution)/shard_map/ppermute | solution.py:99
  210.3 8.9 %collective-permute-start.4 = (f32[4,129,128]{2,1,0:T(8,128)S(1)}, f32[4,129,128]{2,1,0:T(8,128)S(1)}, u32[]{:S(2)}, u32[]{:S(2)}) collective-permute-start(f32[4,129,128]{2,1,0:T(8,128)S(1)} %select_add_fusion.4), channel_id=1, source_target_pairs={{0,64},{4,68},{8,72},{12,76},{16,80},{20,84},{24,88},{28,92},{32,9... | collective-permute-start | bytes 792584 | tf_op jit(solution)/shard_map/ppermute | solution.py:99
  232.9 14.0 %copy-start.19 = (bf16[1024,1,128]{0,2,1:T(8,128)(2,1)S(1)}, bf16[1024,1,128]{0,2,1:T(8,128)(2,1)}, u32[]{:S(2)}) copy-start(bf16[1024,1,128]{0,2,1:T(8,128)(2,1)} %get-tuple-element.86) | copy-start | bytes 786436
  232.9 33.7 %all-to-all-start.3 = ((bf16[32,48,512]{2,1,0:T(8,128)(2,1)}), bf16[32,48,512]{2,1,0:T(8,128)(2,1)S(1)}, u32[]{:S(2)}, u32[]{:S(2)}) async-start(bf16[32,48,512]{2,1,0:T(8,128)(2,1)} %bitcast.39), calls=%async_computation.3 | async-start | bytes 3145728 | tf_op jit(solution)/shard_map/all_to_all | solution.py:120
  243.9 99.8 %all-gather.5.cloned.1.call-start = ((), (), s32[]{:S(2)}) async-start(), calls=%async_computation.5 | async-start | bytes 5242880 | tf_op jit(solution)/shard_map/all_gather | solution.py:122
  247.4 9.2 %copy-start.7 = (bf16[1024,1,128]{2,1,0:T(2,128)(2,1)S(1)}, bf16[1024,1,128]{2,1,0:T(2,128)(2,1)}, u32[]{:S(2)}) copy-start(bf16[1024,1,128]{2,1,0:T(2,128)(2,1)} %get-tuple-element.119) | copy-start | bytes 786436
  247.4 9.2 %copy-start.6 = (bf16[1024,1,128]{2,1,0:T(2,128)(2,1)S(1)}, bf16[1024,1,128]{2,1,0:T(2,128)(2,1)}, u32[]{:S(2)}) copy-start(bf16[1024,1,128]{2,1,0:T(2,128)(2,1)} %get-tuple-element.120) | copy-start | bytes 786436
  249.0 22.7 %collective-permute-start.7 = (f32[4,129,128]{2,1,0:T(8,128)S(1)}, f32[4,129,128]{2,1,0:T(8,128)S(1)}, u32[]{:S(2)}, u32[]{:S(2)}) collective-permute-start(f32[4,129,128]{2,1,0:T(8,128)S(1)} %select_add_fusion.2), channel_id=1, source_target_pairs={{0,16},{4,20},{8,24},{12,28},{16,32},{20,36},{24,40},{28,44},{32,4... | collective-permute-start | bytes 792584 | tf_op jit(solution)/shard_map/ppermute | solution.py:99
  271.7 112.8 %all-gather.7.cloned.1.call-start = ((), (), s32[]{:S(2)}) async-start(), calls=%async_computation.6 | async-start | bytes 5242880 | tf_op jit(solution)/shard_map/all_gather | solution.py:122
  271.8 7.0 %collective-permute-start.8 = (f32[4,129,128]{2,1,0:T(8,128)S(1)}, f32[4,129,128]{2,1,0:T(8,128)S(1)}, u32[]{:S(2)}, u32[]{:S(2)}) collective-permute-start(f32[4,129,128]{2,1,0:T(8,128)S(1)} %select_add_fusion.1), channel_id=1, source_target_pairs={{0,32},{4,36},{8,40},{12,44},{16,48},{20,52},{24,56},{28,60},{32,6... | collective-permute-start | bytes 792584 | tf_op jit(solution)/shard_map/ppermute | solution.py:99
  275.1 10.5 %copy-start.25 = (bf16[1024,1,128]{2,0,1:T(8,128)(2,1)S(1)}, bf16[1024,1,128]{2,0,1:T(8,128)(2,1)}, u32[]{:S(2)}) copy-start(bf16[1024,1,128]{2,0,1:T(8,128)(2,1)} %copy.103) | copy-start | bytes 786436
  278.8 11.4 %collective-permute-start.9 = (f32[4,129,128]{2,1,0:T(8,128)S(1)}, f32[4,129,128]{2,1,0:T(8,128)S(1)}, u32[]{:S(2)}, u32[]{:S(2)}) collective-permute-start(f32[4,129,128]{2,1,0:T(8,128)S(1)} %select_add_fusion), channel_id=1, source_target_pairs={{0,64},{4,68},{8,72},{12,76},{16,80},{20,84},{24,88},{28,92},{32,9... | collective-permute-start | bytes 792584 | tf_op jit(solution)/shard_map/ppermute | solution.py:99
  384.5 10.6 %copy-start.1 = (bf16[1024,1024]{1,0:T(8,128)(2,1)S(1)}, bf16[1024,1024]{1,0:T(8,128)(2,1)}, u32[]{:S(2)}) copy-start(bf16[1024,1024]{1,0:T(8,128)(2,1)} %param.9) | copy-start | bytes 6291460
  (22 other events, 92.6 us)
Sparse Core Ops, SparseCore 0:
  271.8 51.0 all-gather.4
  337.8 46.6 all-gather.6
where the time goes:
time: 410 us; the launch traced here: 402 us
  waiting for transfers between devices  112 us (27%)
  local copies, waits for them, and re-layouts  92.6 us (23%)
  starting transfers between devices  73.5 us (18%)
  matrix products  60.1 us (15%)
  blocking collectives  31.2 us (8%)
  between operations  17.9 us (4%)
  other arithmetic  15.3 us (4%)
    all_to_all x3, waiting for transfers between devices, dispatch(): got = lax.all_to_all(buffer, 'ctx', 0, 0, tiled=True).reshape(slots, width)  63.2 us
    ppermute x10, starting transfers between devices, one_group(): got = lax.ppermute(total, 'ctx', perm)  43.3 us
    all_to_all x1, blocking collectives, one_group(): lax.all_to_all(outgoing, 'ctx', 0, 0, tiled=True)  31.2 us
    all_gather x2, waiting for transfers between devices, one_group(): gathered = lax.all_gather(rows, 'head', axis=1, tiled=True)  30.2 us
    gather x4, local copies, waits for them, and re-layouts, dispatch(): return jnp.take(got, tok_slot, axis=0, mode='clip').reshape(seg, heads, dh)  25.9 us
    dot_general x2, matrix products, one_group(): jnp.dot(gathered, weight_rows[:, first:last].reshape(head_count * group_w...  21.2 us
    all_to_all x3, starting transfers between devices, dispatch(): got = lax.all_to_all(buffer, 'ctx', 0, 0, tiled=True).reshape(slots, width)  19.1 us
    gather x3, local copies, waits for them, and re-layouts, dispatch(): jnp.take(source, slot_row, axis=0, mode='clip').reshape(n, cap, width)  17.5 us
  transfers between devices with their start and end apart: 16, of which 9 were waited for; matrix products, arithmetic and copies ran while one was open for 34% of the time, Pallas kernels for 0%

commit v1 on v0

--- a/solution.py
+++ b/solution.py
@@ -119,7 +119,9 @@
         outgoing = jnp.take(combined, pslot, axis=0, mode="clip").reshape(n, cap, group_width)
         incoming = lax.all_to_all(outgoing, "ctx", 0, 0, tiled=True).reshape(slots, group_width)
         rows = jnp.take(incoming, send_slot, axis=0, mode="clip")
-        gathered = lax.all_gather(rows, "head", axis=1, tiled=True)
+        gathered = jnp.concatenate(
+            lax.all_to_all(jnp.stack([rows] * lax.axis_size("head")), "head", 0, 0), axis=1
+        )
         part = jnp.dot(
             gathered,
             weight_rows[:, first:last].reshape(head_count * group_width, out_cols),

time: 410 us -> 425 us (1.037)
  the two profiles are of different devices: /device:TPU:1 before, /device:TPU:0 now
where the time goes in v1:
time: 425 us; the launch traced here: 417 us
  waiting for transfers between devices  165 us (39%)
  local copies, waits for them, and re-layouts  98.9 us (23%)
  starting transfers between devices  78 us (18%)
  matrix products  57.9 us (14%)
  other arithmetic  13.2 us (3%)
  between operations  4.73 us (1%)
    all_to_all x2, waiting for transfers between devices, one_group(): lax.all_to_all(jnp.stack([rows] * lax.axis_size('head')), 'head', 0, 0)  78 us
    all_to_all x3, waiting for transfers between devices, dispatch(): got = lax.all_to_all(buffer, 'ctx', 0, 0, tiled=True).reshape(slots, width)  62.9 us
    ppermute x10, starting transfers between devices, one_group(): got = lax.ppermute(total, 'ctx', perm)  40.3 us
    gather x4, local copies, waits for them, and re-layouts, dispatch(): return jnp.take(got, tok_slot, axis=0, mode='clip').reshape(seg, heads, dh)  25.9 us
    all_to_all x2, waiting for transfers between devices, one_group(): lax.all_to_all(outgoing, 'ctx', 0, 0, tiled=True)  22.7 us
    dot_general x2, matrix products, one_group(): jnp.dot(gathered, weight_rows[:, first:last].reshape(head_count * group_w...  19.1 us
    all_to_all x3, starting transfers between devices, dispatch(): got = lax.all_to_all(buffer, 'ctx', 0, 0, tiled=True).reshape(slots, width)  17.6 us
    gather x3, local copies, waits for them, and re-layouts, dispatch(): jnp.take(source, slot_row, axis=0, mode='clip').reshape(n, cap, width)  17.4 us
  transfers between devices with their start and end apart: 17, of which 8 were waited for; matrix products, arithmetic and copies ran while one was open for 32% of the time, Pallas kernels for 0%

profile of v1, /device:TPU:0, one launch (start us, length us, event | category | flops | bytes accessed | tf_op | source)
XLA Modules:
  0.0 417.3 jit_solution(16548925400134766208)
XLA Ops:
  2.5 5.8 %gather_fusion.2 = bf16[1536,1024]{1,0:T(8,128)(2,1)} fusion(bf16[1024,1024]{1,0:T(8,128)(2,1)S(1)} %copy-done, s32[2048]{0:T(1024)S(1)} %pad_clamp_fusion.1), kind=kCustom, calls=%fused_computation.2 | custom fusion | bytes 6297600 | tf_op jit(solution)/shard_map/jit(_take)/gather | solution.py:59
  8.3 7.6 %all-to-all-start.1 = ((bf16[32,48,1024]{2,1,0:T(8,128)(2,1)}), bf16[32,48,1024]{2,1,0:T(8,128)(2,1)}, u32[]{:S(2)}, u32[]{:S(2)}) async-start(bf16[32,48,1024]{2,1,0:T(8,128)(2,1)} %bitcast.229), calls=%async_computation.1 | async-start | bytes 6291456 | tf_op jit(solution)/shard_map/all_to_all | solution.py:60
  16.0 5.8 %gather_fusion = bf16[1536,1024]{1,0:T(8,128)(2,1)} fusion(bf16[1024,1024]{1,0:T(8,128)(2,1)S(1)} %copy-done.2, s32[2048]{0:T(1024)S(1)} %pad_clamp_fusion.1), kind=kCustom, calls=%fused_computation | custom fusion | bytes 6297600 | tf_op jit(solution)/shard_map/jit(_take)/gather | solution.py:59
  21.7 34.1 %all-to-all-done.1 = bf16[32,48,1024]{2,1,0:T(8,128)(2,1)} async-done(((bf16[32,48,1024]{2,1,0:T(8,128)(2,1)}), bf16[32,48,1024]{2,1,0:T(8,128)(2,1)}, u32[]{:S(2)}, u32[]{:S(2)}) %all-to-all-start.1) | async-done | bytes 3145760 | tf_op jit(solution)/shard_map/all_to_all | solution.py:60
  64.1 5.8 %gather_fusion.4 = bf16[1536,1024]{1,0:T(8,128)(2,1)} fusion(bf16[1024,1024]{1,0:T(8,128)(2,1)S(1)} %copy-done.3, s32[2048]{0:T(1024)S(1)} %pad_clamp_fusion.1), kind=kCustom, calls=%fused_computation.4 | custom fusion | bytes 6297600 | tf_op jit(solution)/shard_map/jit(_take)/gather | solution.py:59
  72.0 28.8 %all-to-all-done = bf16[32,48,1024]{2,1,0:T(8,128)(2,1)} async-done(((bf16[32,48,1024]{2,1,0:T(8,128)(2,1)}), bf16[32,48,1024]{2,1,0:T(8,128)(2,1)}, u32[]{:S(2)}, u32[]{:S(2)}) %all-to-all-start) | async-done | bytes 3145760 | tf_op jit(solution)/shard_map/all_to_all | solution.py:60
  110.2 8.3 %gather_fusion.3 = bf16[1024,1024]{1,0:T(8,128)(2,1)} fusion(bf16[1536,1024]{1,0:T(8,128)(2,1)} %bitcast.6, s32[1024]{0:T(1024)S(1)} %broadcast_clamp_fusion.1), kind=kCustom, calls=%fused_computation.3 | custom fusion | bytes 4198400 | tf_op jit(solution)/shard_map/jit(_take)/gather | solution.py:61
  122.5 8.3 %gather_fusion.1 = bf16[1024,1024]{1,0:T(8,128)(2,1)} fusion(bf16[1536,1024]{1,0:T(8,128)(2,1)} %bitcast.4, s32[1024]{0:T(1024)S(1)} %broadcast_clamp_fusion.1), kind=kCustom, calls=%fused_computation.1 | custom fusion | bytes 4198400 | tf_op jit(solution)/shard_map/jit(_take)/gather | solution.py:61
  148.5 5.3 %gather_fusion.5 = bf16[1024,1024]{1,0:T(8,128)(2,1)} fusion(bf16[1536,1024]{1,0:T(8,128)(2,1)S(1)} %bitcast.221, s32[1024]{0:T(1024)S(1)} %broadcast_clamp_fusion.1), kind=kCustom, calls=%fused_computation.5 | custom fusion | bytes 4198400 | tf_op jit(solution)/shard_map/jit(_take)/gather | solution.py:61
  201.1 6.2 %collective-permute-start.8 = (f32[4,129,128]{2,1,0:T(8,128)S(1)}, f32[4,129,128]{2,1,0:T(8,128)S(1)}, u32[]{:S(2)}, u32[]{:S(2)}) collective-permute-start(f32[4,129,128]{2,1,0:T(8,128)S(1)} %select_add_fusion.1), channel_id=1, source_target_pairs={{0,32},{4,36},{8,40},{12,44},{16,48},{20,52},{24,56},{28,60},{32,6... | collective-permute-start | bytes 792584 | tf_op jit(solution)/shard_map/ppermute | solution.py:99
  212.9 5.8 %collective-permute-start.4 = (f32[4,129,128]{2,1,0:T(8,128)S(1)}, f32[4,129,128]{2,1,0:T(8,128)S(1)}, u32[]{:S(2)}, u32[]{:S(2)}) collective-permute-start(f32[4,129,128]{2,1,0:T(8,128)S(1)} %select_add_fusion.4), channel_id=1, source_target_pairs={{0,64},{4,68},{8,72},{12,76},{16,80},{20,84},{24,88},{28,92},{32,9... | collective-permute-start | bytes 792584 | tf_op jit(solution)/shard_map/ppermute | solution.py:99
  231.5 5.4 %gather_fusion.6 = bf16[1536,512]{1,0:T(8,128)(2,1)} fusion(bf16[1024,512]{1,0:T(8,128)(2,1)S(1)} %copy.63, s32[2048]{0:T(1024)S(1)} %pad_clamp_fusion), kind=kCustom, calls=%fused_computation.6 | custom fusion | bytes 3151872 | tf_op jit(solution)/shard_map/jit(_take)/gather | solution.py:119
  253.3 5.4 %gather_fusion.8 = bf16[1536,512]{1,0:T(8,128)(2,1)} fusion(bf16[1024,512]{1,0:T(8,128)(2,1)S(1)} %copy.78, s32[2048]{0:T(1024)S(1)} %pad_clamp_fusion), kind=kCustom, calls=%fused_computation.8 | custom fusion | bytes 3151872 | tf_op jit(solution)/shard_map/jit(_take)/gather | solution.py:119
  258.8 6.3 %all-to-all-done.3 = bf16[32,48,512]{2,1,0:T(8,128)(2,1)S(1)} async-done(((bf16[32,48,512]{2,1,0:T(8,128)(2,1)}), bf16[32,48,512]{2,1,0:T(8,128)(2,1)S(1)}, u32[]{:S(2)}, u32[]{:S(2)}) %all-to-all-start.3) | async-done | bytes 1572896 | tf_op jit(solution)/shard_map/all_to_all | solution.py:120
  269.8 5.1 %gather_fusion.7 = bf16[1024,512]{1,0:T(8,128)(2,1)} fusion(bf16[1536,512]{1,0:T(8,128)(2,1)S(1)} %bitcast.222, s32[1024]{0:T(1024)S(1)} %broadcast_clamp_fusion), kind=kCustom, calls=%fused_computation.7 | custom fusion | bytes 2101248 | tf_op jit(solution)/shard_map/jit(_take)/gather | solution.py:121
  276.4 16.5 %all-to-all-done.5 = bf16[32,48,512]{2,1,0:T(8,128)(2,1)} async-done(((bf16[32,48,512]{2,1,0:T(8,128)(2,1)}), bf16[32,48,512]{2,1,0:T(8,128)(2,1)}, u32[]{:S(2)}, u32[]{:S(2)}) %all-to-all-start.5) | async-done | bytes 1572896 | tf_op jit(solution)/shard_map/all_to_all | solution.py:120
  295.4 5.3 %all-to-all-start.4 = ((bf16[4,1024,512]{1,2,0:T(8,128)(2,1)}), bf16[4,1024,512]{1,2,0:T(8,128)(2,1)}, u32[]{:S(2)}, u32[]{:S(2)}) async-start(bf16[4,1024,512]{1,2,0:T(8,128)(2,1)} %stack.4), calls=%async_computation.4 | async-start | bytes 8388608 | tf_op jit(solution)/shard_map/all_to_all | solution.py:123
  300.7 5.6 %gather_fusion.9 = bf16[1024,512]{1,0:T(8,128)(2,1)S(1)} fusion(bf16[1536,512]{1,0:T(8,128)(2,1)} %bitcast.77, s32[1024]{0:T(1024)S(1)} %broadcast_clamp_fusion), kind=kCustom, calls=%fused_computation.9 | custom fusion | bytes 2101248 | tf_op jit(solution)/shard_map/jit(_take)/gather | solution.py:121
  306.8 43.3 %all-to-all-done.4 = bf16[4,1024,512]{1,2,0:T(8,128)(2,1)} async-done(((bf16[4,1024,512]{1,2,0:T(8,128)(2,1)}), bf16[4,1024,512]{1,2,0:T(8,128)(2,1)}, u32[]{:S(2)}, u32[]{:S(2)}) %all-to-all-start.4) | async-done | bytes 4194336 | tf_op jit(solution)/shard_map/all_to_all | solution.py:123
  352.6 5.1 %all-to-all-start.6 = ((bf16[4,1024,512]{1,2,0:T(8,128)(2,1)}), bf16[4,1024,512]{1,2,0:T(8,128)(2,1)}, u32[]{:S(2)}, u32[]{:S(2)}) async-start(bf16[4,1024,512]{1,2,0:T(8,128)(2,1)} %stack.5), calls=%async_computation.6 | async-start | bytes 8388608 | tf_op jit(solution)/shard_map/all_to_all | solution.py:123
  357.8 5.3 %fusion.164 = (bf16[4,4,128,1024]{3,2,1,0:T(8,128)(2,1)}, bf16[4,4,128,1024]{3,2,1,0:T(8,128)(2,1)S(1)}) fusion(bf16[4,8,128,1024]{3,2,1,0:T(8,128)(2,1)} %bitcast.232), kind=kLoop, calls=%fused_computation.258 | loop fusion | bytes 16777216 | tf_op jit(solution)/shard_map/slice | solution.py:127
  363.0 8.4 %fusion.171 = f32[1024,1024]{1,0:T(8,128)} fusion(bf16[1024,2048]{0,1:T(8,128)(2,1)} %bitcast.45, bf16[2048,1024]{1,0:T(8,128)(2,1)S(1)} %bitcast.239), kind=kOutput, calls=%fused_computation.265 | convolution fusion | flops 4294967296 | bytes 12582912 | tf_op jit(solution)/shard_map/dot_general | solution.py:125
  371.4 34.7 %all-to-all-done.6 = bf16[4,1024,512]{1,2,0:T(8,128)(2,1)} async-done(((bf16[4,1024,512]{1,2,0:T(8,128)(2,1)}), bf16[4,1024,512]{1,2,0:T(8,128)(2,1)}, u32[]{:S(2)}, u32[]{:S(2)}) %all-to-all-start.6) | async-done | bytes 4194336 | tf_op jit(solution)/shard_map/all_to_all | solution.py:123
  406.1 10.7 %add_convert_fusion = bf16[1024,1024]{1,0:T(8,128)(2,1)} fusion(f32[1024,1024]{1,0:T(8,128)} %fusion.171, bf16[1024,2048]{0,1:T(8,128)(2,1)} %bitcast.79, bf16[2048,1024]{1,0:T(8,128)(2,1)} %bitcast.238), kind=kOutput, calls=%fused_computation.26 | convolution fusion | flops 4297064448 | bytes 14680064 | tf_op jit(solution)/shard_map/dot_general | solution.py:125
  (192 shorter events, 133.6 us)
Async XLA Ops:
  8.3 7.7 %copy-start.2 = (bf16[1024,1024]{1,0:T(8,128)(2,1)S(1)}, bf16[1024,1024]{1,0:T(8,128)(2,1)}, u32[]{:S(2)}) copy-start(bf16[1024,1024]{1,0:T(8,128)(2,1)} %param.8) | copy-start | bytes 6291460
  8.3 47.6 %all-to-all-start.1 = ((bf16[32,48,1024]{2,1,0:T(8,128)(2,1)}), bf16[32,48,1024]{2,1,0:T(8,128)(2,1)}, u32[]{:S(2)}, u32[]{:S(2)}) async-start(bf16[32,48,1024]{2,1,0:T(8,128)(2,1)} %bitcast.229), calls=%async_computation.1 | async-start | bytes 6291456 | tf_op jit(solution)/shard_map/all_to_all | solution.py:60
  21.7 39.1 %copy-start.31 = (s32[32]{0:T(128)S(1)}, s32[32]{0:T(128)}, u32[]{:S(2)}) copy-start(s32[32]{0:T(128)} %param.11) | copy-start | bytes 388
  21.7 42.4 %copy-start.3 = (bf16[1024,1024]{1,0:T(8,128)(2,1)S(1)}, bf16[1024,1024]{1,0:T(8,128)(2,1)}, u32[]{:S(2)}) copy-start(bf16[1024,1024]{1,0:T(8,128)(2,1)} %param.7) | copy-start | bytes 6291460
  55.9 44.9 %all-to-all-start = ((bf16[32,48,1024]{2,1,0:T(8,128)(2,1)}), bf16[32,48,1024]{2,1,0:T(8,128)(2,1)}, u32[]{:S(2)}, u32[]{:S(2)}) async-start(bf16[32,48,1024]{2,1,0:T(8,128)(2,1)} %bitcast.228), calls=%async_computation | async-start | bytes 6291456 | tf_op jit(solution)/shard_map/all_to_all | solution.py:60
  100.7 47.7 %all-to-all-start.2 = ((bf16[32,48,1024]{2,1,0:T(8,128)(2,1)}), bf16[32,48,1024]{2,1,0:T(8,128)(2,1)S(1)}, u32[]{:S(2)}, u32[]{:S(2)}) async-start(bf16[32,48,1024]{2,1,0:T(8,128)(2,1)} %bitcast.227), calls=%async_computation.2 | async-start | bytes 6291456 | tf_op jit(solution)/shard_map/all_to_all | solution.py:60
  160.2 11.8 %collective-permute-start = (f32[4,129,128]{2,1,0:T(8,128)S(1)}, f32[4,129,128]{2,1,0:T(8,128)S(1)}, u32[]{:S(2)}, u32[]{:S(2)}) collective-permute-start(f32[4,129,128]{2,1,0:T(8,128)S(1)} %pad_maximum_fusion), channel_id=1, source_target_pairs={{0,4},{4,8},{8,12},{12,16},{16,20},{20,24},{24,28},{28,32},{32,36}... | collective-permute-start | bytes 792584 | tf_op jit(solution)/shard_map/ppermute | solution.py:99
  162.7 12.8 %collective-permute-start.5 = (f32[4,129,128]{2,1,0:T(8,128)S(1)}, f32[4,129,128]{2,1,0:T(8,128)S(1)}, u32[]{:S(2)}, u32[]{:S(2)}) collective-permute-start(f32[4,129,128]{2,1,0:T(8,128)S(1)} %pad_maximum_fusion.1), channel_id=1, source_target_pairs={{0,4},{4,8},{8,12},{12,16},{16,20},{20,24},{24,28},{28,32},{32,36}... | collective-permute-start | bytes 792584 | tf_op jit(solution)/shard_map/ppermute | solution.py:99
  172.0 12.4 %collective-permute-start.1 = (f32[4,129,128]{2,1,0:T(8,128)S(1)}, f32[4,129,128]{2,1,0:T(8,128)S(1)}, u32[]{:S(2)}, u32[]{:S(2)}) collective-permute-start(f32[4,129,128]{2,1,0:T(8,128)S(1)} %select_add_fusion.7), channel_id=1, source_target_pairs={{0,8},{4,12},{8,16},{12,20},{16,24},{20,28},{24,32},{28,36},{32,40... | collective-permute-start | bytes 792584 | tf_op jit(solution)/shard_map/ppermute | solution.py:99
  175.5 14.0 %collective-permute-start.6 = (f32[4,129,128]{2,1,0:T(8,128)S(1)}, f32[4,129,128]{2,1,0:T(8,128)S(1)}, u32[]{:S(2)}, u32[]{:S(2)}) collective-permute-start(f32[4,129,128]{2,1,0:T(8,128)S(1)} %select_add_fusion.3), channel_id=1, source_target_pairs={{0,8},{4,12},{8,16},{12,20},{16,24},{20,28},{24,32},{28,36},{32,40... | collective-permute-start | bytes 792584 | tf_op jit(solution)/shard_map/ppermute | solution.py:99
  184.4 11.6 %copy-start.9 = (bf16[1024,1,128]{2,1,0:T(2,128)(2,1)S(1)}, bf16[1024,1,128]{2,1,0:T(2,128)(2,1)}, u32[]{:S(2)}) copy-start(bf16[1024,1,128]{2,1,0:T(2,128)(2,1)} %get-tuple-element.119) | copy-start | bytes 786436
  184.5 12.1 %collective-permute-start.2 = (f32[4,129,128]{2,1,0:T(8,128)S(1)}, f32[4,129,128]{2,1,0:T(8,128)S(1)}, u32[]{:S(2)}, u32[]{:S(2)}) collective-permute-start(f32[4,129,128]{2,1,0:T(8,128)S(1)} %select_add_fusion.6), channel_id=1, source_target_pairs={{0,16},{4,20},{8,24},{12,28},{16,32},{20,36},{24,40},{28,44},{32,4... | collective-permute-start | bytes 792584 | tf_op jit(solution)/shard_map/ppermute | solution.py:99
  189.6 11.5 %collective-permute-start.7 = (f32[4,129,128]{2,1,0:T(8,128)S(1)}, f32[4,129,128]{2,1,0:T(8,128)S(1)}, u32[]{:S(2)}, u32[]{:S(2)}) collective-permute-start(f32[4,129,128]{2,1,0:T(8,128)S(1)} %select_add_fusion.2), channel_id=1, source_target_pairs={{0,16},{4,20},{8,24},{12,28},{16,32},{20,36},{24,40},{28,44},{32,4... | collective-permute-start | bytes 792584 | tf_op jit(solution)/shard_map/ppermute | solution.py:99
  196.6 16.3 %collective-permute-start.3 = (f32[4,129,128]{2,1,0:T(8,128)S(1)}, f32[4,129,128]{2,1,0:T(8,128)S(1)}, u32[]{:S(2)}, u32[]{:S(2)}) collective-permute-start(f32[4,129,128]{2,1,0:T(8,128)S(1)} %select_add_fusion.5), channel_id=1, source_target_pairs={{0,32},{4,36},{8,40},{12,44},{16,48},{20,52},{24,56},{28,60},{32,6... | collective-permute-start | bytes 792584 | tf_op jit(solution)/shard_map/ppermute | solution.py:99
  201.1 7.5 %copy-start.18 = (bf16[1024,1,128]{0,2,1:T(8,128)(2,1)S(1)}, bf16[1024,1,128]{0,2,1:T(8,128)(2,1)}, u32[]{:S(2)}) copy-start(bf16[1024,1,128]{0,2,1:T(8,128)(2,1)} %get-tuple-element.67) | copy-start | bytes 786436
  201.1 17.6 %collective-permute-start.8 = (f32[4,129,128]{2,1,0:T(8,128)S(1)}, f32[4,129,128]{2,1,0:T(8,128)S(1)}, u32[]{:S(2)}, u32[]{:S(2)}) collective-permute-start(f32[4,129,128]{2,1,0:T(8,128)S(1)} %select_add_fusion.1), channel_id=1, source_target_pairs={{0,32},{4,36},{8,40},{12,44},{16,48},{20,52},{24,56},{28,60},{32,6... | collective-permute-start | bytes 792584 | tf_op jit(solution)/shard_map/ppermute | solution.py:99
  212.9 12.2 %collective-permute-start.4 = (f32[4,129,128]{2,1,0:T(8,128)S(1)}, f32[4,129,128]{2,1,0:T(8,128)S(1)}, u32[]{:S(2)}, u32[]{:S(2)}) collective-permute-start(f32[4,129,128]{2,1,0:T(8,128)S(1)} %select_add_fusion.4), channel_id=1, source_target_pairs={{0,64},{4,68},{8,72},{12,76},{16,80},{20,84},{24,88},{28,92},{32,9... | collective-permute-start | bytes 792584 | tf_op jit(solution)/shard_map/ppermute | solution.py:99
  218.8 26.2 %collective-permute-start.9 = (f32[4,129,128]{2,1,0:T(8,128)S(1)}, f32[4,129,128]{2,1,0:T(8,128)}, u32[]{:S(2)}, u32[]{:S(2)}) collective-permute-start(f32[4,129,128]{2,1,0:T(8,128)S(1)} %select_add_fusion), channel_id=1, source_target_pairs={{0,64},{4,68},{8,72},{12,76},{16,80},{20,84},{24,88},{28,92},{32,9... | collective-permute-start | bytes 792584 | tf_op jit(solution)/shard_map/ppermute | solution.py:99
  236.9 28.2 %all-to-all-start.3 = ((bf16[32,48,512]{2,1,0:T(8,128)(2,1)}), bf16[32,48,512]{2,1,0:T(8,128)(2,1)S(1)}, u32[]{:S(2)}, u32[]{:S(2)}) async-start(bf16[32,48,512]{2,1,0:T(8,128)(2,1)} %bitcast.236), calls=%async_computation.3 | async-start | bytes 3145728 | tf_op jit(solution)/shard_map/all_to_all | solution.py:120
  253.3 16.4 %copy-start.24 = (s32[1024]{0:T(1024)S(1)}, s32[1024]{0:T(1024)}, u32[]{:S(2)}) copy-start(s32[1024]{0:T(1024)} %copy-done.23) | copy-start | bytes 12292
  265.0 27.8 %all-to-all-start.5 = ((bf16[32,48,512]{2,1,0:T(8,128)(2,1)}), bf16[32,48,512]{2,1,0:T(8,128)(2,1)}, u32[]{:S(2)}, u32[]{:S(2)}) async-start(bf16[32,48,512]{2,1,0:T(8,128)(2,1)} %bitcast.237), calls=%async_computation.5 | async-start | bytes 3145728 | tf_op jit(solution)/shard_map/all_to_all | solution.py:120
  295.4 54.8 %all-to-all-start.4 = ((bf16[4,1024,512]{1,2,0:T(8,128)(2,1)}), bf16[4,1024,512]{1,2,0:T(8,128)(2,1)}, u32[]{:S(2)}, u32[]{:S(2)}) async-start(bf16[4,1024,512]{1,2,0:T(8,128)(2,1)} %stack.4), calls=%async_computation.4 | async-start | bytes 8388608 | tf_op jit(solution)/shard_map/all_to_all | solution.py:123
  352.6 53.5 %all-to-all-start.6 = ((bf16[4,1024,512]{1,2,0:T(8,128)(2,1)}), bf16[4,1024,512]{1,2,0:T(8,128)(2,1)}, u32[]{:S(2)}, u32[]{:S(2)}) async-start(bf16[4,1024,512]{1,2,0:T(8,128)(2,1)} %stack.5), calls=%async_computation.6 | async-start | bytes 8388608 | tf_op jit(solution)/shard_map/all_to_all | solution.py:123
  406.1 10.7 %copy-start.1 = (bf16[1024,1024]{1,0:T(8,128)(2,1)S(1)}, bf16[1024,1024]{1,0:T(8,128)(2,1)}, u32[]{:S(2)}) copy-start(bf16[1024,1024]{1,0:T(8,128)(2,1)} %param.9) | copy-start | bytes 6291460
  (28 other events, 101.5 us)
